TPU v7x, 32 devices: a whole 2x2x4 slice. The times are simulated.
32 devices in a mesh: cuts: 8 (over y, x, core), row: 4 (over z).
Axes of the slice: x: 2, y: 2, z: 4, core: 2. Of those that a mesh axis runs over, the one named last changes fastest.
Arguments:
- vectors: bfloat16 [8, 128, 98304], P('cuts', None, 'row'), may hold values from -100 to 100
- counts: int32 [8], P('cuts'), may hold values from 64 to 128, as said below
- offsets: int32 [8, 2], P('cuts'), may hold values from 0 to 96, as said below
- margin_blocks: bfloat16 [1024, 96, 288], P('row'), may hold values from -0.5 to 1.5
- energy_blocks: bfloat16 [1024, 96, 288], P('row'), may hold values from -1 to 6
- block_columns: int32 [1024, 3], P('row'), may hold values from 0 to 1023, as said below
Outputs:
- ritz_residual: bfloat16 [8, 128, 98304], P('cuts', None, 'row')
- margin_pencil: float32 [8, 128, 128], P('cuts')
- energy_pencil: float32 [8, 128, 128], P('cuts')
Inputs may be any that keep to these rules, and one draw needn't show every extreme that they name: `counts`: some slice has all 128 vectors valid and another exactly 64. offsets[s, 0] is at most 8; offsets[s, 1] + 32 lies between counts[s] - 8 and counts[s]; so both windows lie among the valid vectors. block_columns[i, 0] = i, block_columns[i, 1] lies in i - 2 to i and block_columns[i, 2] in i to i + 2.
All inputs are finite; a program needn't handle non-finite values.
Results may differ from a plain program's by a relative error of at most 0.00225.
The roundings to bfloat16 on the way count: a program that leaves them out, or rounds other values in their place, can miss the bound.
Values may be sent and summed in bfloat16 or wider, within the bound.
No kernel may reach another device: no remote copies, remote signals or barrier semaphores. Data moves between devices by JAX's collectives and lax.ppermute only.
A program may use at most 256 MiB of HBM per device.

v0:
```python
import jax
import jax.numpy as jnp
from jax import lax
from jax.sharding import PartitionSpec as P

NMAT = 98304
WIN = 32


def from_behind(block, axis, distance):
    devices = range(lax.axis_size(axis))
    route = [(i - distance, i) for i in devices if i - distance in devices]
    return lax.ppermute(block, axis, route)


def padded_2(cells, sides, width):
    for axis, dim in sides:
        count = lax.axis_size(axis)
        ends = count - 1
        head = lax.slice_in_dim(cells, 0, width, axis=dim)
        tail = lax.slice_in_dim(cells, cells.shape[dim] - width, cells.shape[dim], axis=dim)
        cells = jnp.concatenate(
            [
                lax.ppermute(tail, axis, [(i, (i + 1) % count) for i in range(ends)]),
                cells,
                lax.ppermute(head, axis, [((i + 1) % count, i) for i in range(ends)]),
            ],
            axis=dim,
        )
    return cells


def block_product(matrices, shifts, padded):
    width = padded.shape[0]
    block_rows = shifts.shape[0]
    size_block = matrices[0].shape[1]
    grid = padded.reshape(width, block_rows + 4, size_block)
    centre = grid[:, 2 : 2 + block_rows]
    choices_of = ((0,), (-2, -1, 0), (0, 1, 2))
    picked_all = []
    for column_slot in range(len(choices_of)):
        picked = centre
        for distance in choices_of[column_slot]:
            if distance != 0:
                view = grid[:, 2 + distance : 2 + distance + block_rows]
                hit = (shifts[:, column_slot] == distance)[None, :, None]
                picked = jnp.where(hit, view, picked)
        picked_all.append(picked)
    results = []
    for blocks in matrices:
        total = None
        for column_slot in range(len(choices_of)):
            part_blocks = blocks[:, :, column_slot * size_block : (column_slot + 1) * size_block]
            term = jnp.einsum(
                "cnb,nab->cna",
                picked_all[column_slot],
                part_blocks,
                preferred_element_type=jnp.float32,
            )
            total = term if total is None else total + term
        results.append(total.reshape(width, block_rows * size_block).astype(jnp.bfloat16))
    return results


def shards(vectors, counts, offsets, margin_blocks, energy_blocks, block_columns):
    own_vectors = vectors[0]
    vector_count = own_vectors.shape[0]
    block_rows = margin_blocks.shape[0]
    size_block = margin_blocks.shape[1]
    rim_width = 2 * size_block
    valid_mask = jnp.arange(vector_count, dtype=jnp.int32) < counts[0]
    masked = jnp.where(valid_mask[:, None], own_vectors, jnp.zeros((), own_vectors.dtype))
    lower_window = lax.dynamic_slice_in_dim(masked, offsets[0, 0], WIN, 0)
    upper_window = lax.dynamic_slice_in_dim(masked, offsets[0, 1], WIN, 0)
    own_blocks = lax.axis_index("row") * block_rows + jnp.arange(block_rows, dtype=jnp.int32)
    shifts = block_columns - own_blocks[:, None]
    from_below = [from_behind(upper_window, "cuts", distance) for distance in (2, 1)]
    from_above = [from_behind(lower_window, "cuts", -distance) for distance in (1, 2)]
    windows = jnp.concatenate(from_below + from_above, axis=0)
    padded_windows = padded_2(windows, (("row", 1),), rim_width)
    margin_windows = block_product((margin_blocks,), shifts, padded_windows)[0]
    partial_margin = jnp.dot(margin_windows, masked.T, preferred_element_type=jnp.float32)
    margin = lax.psum(partial_margin, "row") / NMAT
    removed = jnp.dot(margin.astype(jnp.bfloat16).T, windows, preferred_element_type=jnp.float32)
    cleaned = (masked.astype(jnp.float32) - removed).astype(jnp.bfloat16)
    padded_cleaned = padded_2(cleaned, (("row", 1),), rim_width)
    margin_cleaned, energy_cleaned = block_product(
        (margin_blocks, energy_blocks), shifts, padded_cleaned
    )
    margin_part = jnp.dot(cleaned, margin_cleaned.T, preferred_element_type=jnp.float32)
    energy_part = jnp.dot(cleaned, energy_cleaned.T, preferred_element_type=jnp.float32)
    margin_total, energy_total = lax.psum((margin_part, energy_part), "row")
    margin_pencil = margin_total / NMAT
    energy_pencil = energy_total / NMAT
    margin_diag = jnp.diagonal(margin_pencil)
    energy_diag = jnp.diagonal(energy_pencil)
    theta = jnp.where(
        valid_mask,
        energy_diag / jnp.where(valid_mask, margin_diag, jnp.float32(1.0)),
        jnp.float32(0.0),
    )
    residual = (
        energy_cleaned.astype(jnp.float32) - theta[:, None] * margin_cleaned.astype(jnp.float32)
    ).astype(jnp.bfloat16)
    return (residual[None], margin_pencil[None], energy_pencil[None])


def solution(mesh):
    placed = (
        P("cuts", None, "row"),
        P("cuts"),
        P("cuts", None),
        P("row", None, None),
        P("row", None, None),
        P("row", None),
    )
    return jax.shard_map(
        shards,
        mesh=mesh,
        in_specs=placed,
        out_specs=(P("cuts", None, "row"), P("cuts", None, None), P("cuts", None, None)),
        check_vma=False,
    )
```

profile of v0, /device:TPU:0, one launch (start us, length us, event | category | flops | bytes accessed | tf_op | source)
XLA Modules:
  0.0 498.3 jit_solution(1936045789571381187)
XLA Ops:
  7.2 0.0 all-reduce.4.cloned.1.call-start
  7.2 1.3 fusion.39
  13.1 3.3 bitcast_select_fusion
  16.3 2.6 copy-done.3
  19.0 2.5 constant_dynamic-slice_fusion
  21.4 6.0 %collective-permute-start = (bf16[32,24576]{1,0:T(8,128)(2,1)}, bf16[32,24576]{1,0:T(8,128)(2,1)}, u32[]{:S(2)}, u32[]{:S(2)}) collective-permute-start(bf16[32,24576]{1,0:T(8,128)(2,1)} %get-tuple-element.22), channel_id=1, source_target_pairs={{0,8},{4,12},{8,16},{12,20},{16,24},{20,28},{1,9},{5,13},{9,17},{1... | collective-permute-start | bytes 4718600 | tf_op jit(solution)/shard_map/ppermute | solution.py:13
  27.5 2.6 collective-permute-start.1
  30.1 1.3 collective-permute-start.2
  31.4 1.3 collective-permute-start.3
  32.7 10.8 %fusion.36 = (bf16[256,96,96]{0,2,1:T(8,128)(2,1)}, bf16[256,96,96]{0,2,1:T(8,128)(2,1)}, bf16[256,96,96]{0,2,1:T(8,128)(2,1)}) fusion(bf16[256,96,288]{0,2,1:T(8,128)(2,1)} %param.9), kind=kLoop, calls=%fused_computation.64 | loop fusion | bytes 28311552 | tf_op jit(solution)/shard_map/slice | solution.py:53
  43.5 17.8 %collective-permute-done = bf16[32,24576]{1,0:T(8,128)(2,1)} collective-permute-done((bf16[32,24576]{1,0:T(8,128)(2,1)}, bf16[32,24576]{1,0:T(8,128)(2,1)}, u32[]{:S(2)}, u32[]{:S(2)}) %collective-permute-start) | collective-permute-done | bytes 1572896 | tf_op jit(solution)/shard_map/ppermute | solution.py:13
  61.4 1.5 constant_dynamic-update-slice_fusion.3
  62.9 0.0 collective-permute-done.1
  62.9 1.5 constant_dynamic-update-slice_fusion.2
  64.4 0.1 constant_dynamic-update-slice_fusion.1
  64.5 64.9 %collective-permute-done.3 = bf16[32,24576]{1,0:T(8,128)(2,1)S(1)} collective-permute-done((bf16[32,24576]{1,0:T(8,128)(2,1)}, bf16[32,24576]{1,0:T(8,128)(2,1)S(1)}, u32[]{:S(2)}, u32[]{:S(2)}) %collective-permute-start.3) | collective-permute-done | bytes 1572896 | tf_op jit(solution)/shard_map/ppermute | solution.py:13
  129.5 0.1 constant_dynamic-update-slice_fusion
  129.6 0.0 copy-start.4
  129.6 2.7 copy-done.4
  132.3 0.1 fusion.38
  132.4 3.5 collective-permute-start.4
  135.9 1.3 collective-permute-start.5
  137.2 8.4 %copy.31 = bf16[256,96,96]{2,1,0:T(8,128)(2,1)} copy(bf16[256,96,96]{0,2,1:T(8,128)(2,1)} %get-tuple-element.13) | data formatting | bytes 9437184
  145.6 8.4 %copy.30 = bf16[256,96,96]{2,1,0:T(8,128)(2,1)} copy(bf16[256,96,96]{0,2,1:T(8,128)(2,1)} %get-tuple-element.14) | data formatting | bytes 9437184
  154.1 8.5 %copy.32 = bf16[256,96,96]{2,1,0:T(8,128)(2,1)} copy(bf16[256,96,96]{0,2,1:T(8,128)(2,1)} %get-tuple-element.12) | data formatting | bytes 9437184
  162.5 13.5 %concatenate.15 = bf16[128,24960]{1,0:T(8,128)(2,1)} concatenate(bf16[128,192]{1,0:T(8,128)(2,1)S(1)} %collective-permute-done.4, bf16[128,24576]{1,0:T(8,128)(2,1)} %copy-done.4, bf16[128,192]{1,0:T(8,128)(2,1)S(1)} %collective-permute-done.5), dimensions={1} | concatenate | bytes 12779520 | tf_op jit(solution)/shard_map/concatenate | solution.py:22
  176.0 9.2 %copy.19 = bf16[128,24960]{0,1:T(8,128)(2,1)} copy(bf16[128,24960]{1,0:T(8,128)(2,1)} %concatenate.15) | data formatting | bytes 12779520 | tf_op jit(solution)/shard_map/concatenate | solution.py:22
  185.2 11.1 %fusion.21 = f32[256,128,96]{1,2,0:T(8,128)} fusion(bf16[256,96,96]{2,1,0:T(8,128)(2,1)} %copy.30, bf16[128,260,96]{0,2,1:T(8,128)(2,1)} %bitcast.69), kind=kOutput, calls=%fused_computation.33 | convolution fusion | flops 603979776 | bytes 25165824 | tf_op jit(solution)/shard_map/cnb,nab->cna/dot_general | solution.py:54
  196.3 14.7 %fusion.8 = f32[256,128,96]{1,2,0:T(8,128)} fusion(bf16[256,96,96]{2,1,0:T(8,128)(2,1)} %copy.31, bf16[128,260,96]{0,2,1:T(8,128)(2,1)} %bitcast.70, pred[256]{0:T(512)(128)(4,1)S(1)} %get-tuple-element.4, pred[256]{0:T(512)(128)(4,1)S(1)} %get-tuple-element.6), kind=kOutput, calls=%fused_computation.18 | convolution fusion | flops 610271232 | bytes 37749248 | tf_op jit(solution)/shard_map/cnb,nab->cna/dot_general | solution.py:54
  211.1 18.4 %add_convert_fusion.2 = bf16[256,128,96]{1,2,0:T(8,128)(2,1)} fusion(f32[256,128,96]{1,2,0:T(8,128)} %fusion.21, f32[256,128,96]{1,2,0:T(8,128)} %fusion.8, bf16[256,96,96]{2,1,0:T(8,128)(2,1)S(1)} %bitcast.68, bf16[128,260,96]{0,2,1:T(8,128)(2,1)} %bitcast.71, pred[256]{0:T(512)(128)(4,1)S(1)} %get-tuple-element.5, pred[256]{0:T(512)(128)(4,1)S(1)} %get-tuple-element.3), kind=kOutput, calls=%fused_computation.7 | convolution fusion | flops 619708416 | bytes 55050752 | tf_op jit(solution)/shard_map/cnb,nab->cna/dot_general | solution.py:54
  229.5 7.2 %fusion.11 = f32[128,128]{1,0:T(8,128)} fusion(bf16[128,24576]{0,1:T(8,128)(2,1)} %bitcast.72, bf16[1,128,24576]{2,1,0:T(8,128)(2,1)} %param.6, pred[128]{0:T(512)(128)(4,1)S(1)} %iota_compare_fusion), kind=kOutput, calls=%fused_computation.22 | convolution fusion | flops 808452096 | bytes 12648576 | tf_op jit(solution)/shard_map/dot_general | solution.py:82
  236.7 0.0 all-reduce.4.cloned.1.call-update
  236.7 0.2 all-reduce.6.cloned.1.call-start
  236.9 10.8 %fusion.35 = (bf16[256,96,96]{0,2,1:T(8,128)(2,1)}, bf16[256,96,96]{0,2,1:T(8,128)(2,1)}, bf16[256,96,96]{0,2,1:T(8,128)(2,1)}) fusion(bf16[256,96,288]{0,2,1:T(8,128)(2,1)} %param.10), kind=kLoop, calls=%fused_computation.63 | loop fusion | bytes 28311552 | tf_op jit(solution)/shard_map/slice | solution.py:53
  247.7 24.5 %all-reduce.4.cloned.1.call-done = f32[128,128]{1,0:T(8,128)} async-done(((f32[128,128]{1,0:T(8,128)}), f32[128,128]{1,0:T(8,128)}) %all-reduce.4.cloned.1.call-update) | async-done | bytes 65552 | tf_op jit(solution)/shard_map/psum | solution.py:83
  272.2 6.4 %fusion = bf16[128,24576]{1,0:T(8,128)(2,1)S(1)} fusion(bf16[128,24576]{1,0:T(8,128)(2,1)} %copy-done.4, bf16[128,24576]{1,0:T(8,128)(2,1)} %copy-done.3, f32[128,128]{1,0:T(8,128)} %all-reduce.4.cloned.1.call-done), kind=kOutput, calls=%fused_computation.3 | convolution fusion | flops 814776320 | bytes 18939904 | tf_op jit(solution)/shard_map/dot_general | solution.py:84
  278.6 2.6 copy-done.1
  281.2 0.1 fusion.37
  281.3 3.3 collective-permute-start.6
  284.7 1.3 collective-permute-start.7
  286.0 8.4 %copy.33 = bf16[256,96,96]{2,1,0:T(8,128)(2,1)} copy(bf16[256,96,96]{0,2,1:T(8,128)(2,1)} %get-tuple-element.10) | data formatting | bytes 9437184
  294.4 8.3 %copy.29 = bf16[256,96,96]{2,1,0:T(8,128)(2,1)} copy(bf16[256,96,96]{0,2,1:T(8,128)(2,1)} %get-tuple-element.11) | data formatting | bytes 9437184
  302.7 8.5 %copy.34 = bf16[256,96,96]{2,1,0:T(8,128)(2,1)} copy(bf16[256,96,96]{0,2,1:T(8,128)(2,1)} %get-tuple-element.9) | data formatting | bytes 9437184
  311.2 13.5 %concatenate.16 = bf16[128,24960]{1,0:T(8,128)(2,1)} concatenate(bf16[128,192]{1,0:T(8,128)(2,1)S(1)} %collective-permute-done.6, bf16[128,24576]{1,0:T(8,128)(2,1)} %copy-done.1, bf16[128,192]{1,0:T(8,128)(2,1)S(1)} %collective-permute-done.7), dimensions={1} | concatenate | bytes 12779520 | tf_op jit(solution)/shard_map/concatenate | solution.py:22
  324.6 9.2 %copy.23 = bf16[128,24960]{0,1:T(8,128)(2,1)} copy(bf16[128,24960]{1,0:T(8,128)(2,1)} %concatenate.16) | data formatting | bytes 12779520 | tf_op jit(solution)/shard_map/concatenate | solution.py:22
  333.9 13.8 %fusion.1 = (bf16[128,256,96]{0,2,1:T(8,128)(2,1)}, bf16[128,256,96]{0,2,1:T(8,128)(2,1)S(1)}) fusion(bf16[128,260,96]{0,2,1:T(8,128)(2,1)} %bitcast.56, pred[256]{0:T(512)(128)(4,1)S(1)} %get-tuple-element.5, pred[256]{0:T(512)(128)(4,1)S(1)} %get-tuple-element.3, pred[256]{0:T(512)(128)(4,1)S(1)} %get-tuple-element.4, pred[256]{0:T(512)(128)(4,1)S(1)} %get-tuple-element.6), kind=kLoop, calls=%fused_computation.9 | loop fusion | flops 12582912 | bytes 44041216 | tf_op jit(solution)/shard_map/jit(_where)/select_n | solution.py:47
  347.7 11.4 %fusion.25 = f32[256,128,96]{1,2,0:T(8,128)} fusion(bf16[256,96,96]{2,1,0:T(8,128)(2,1)} %copy.30, bf16[128,260,96]{0,2,1:T(8,128)(2,1)S(1)} %bitcast.57), kind=kOutput, calls=%fused_computation.37 | convolution fusion | flops 603979776 | bytes 23592960 | tf_op jit(solution)/shard_map/cnb,nab->cna/dot_general | solution.py:54
  359.1 9.1 %fusion.43 = f32[256,128,96]{1,2,0:T(8,128)} fusion(bf16[256,96,96]{2,1,0:T(8,128)(2,1)} %copy.31, bf16[128,256,96]{0,2,1:T(8,128)(2,1)S(1)} %get-tuple-element.16), kind=kOutput, calls=%fused_computation.71 | convolution fusion | flops 603979776 | bytes 23592960 | tf_op jit(solution)/shard_map/cnb,nab->cna/dot_general | solution.py:54
  368.3 15.8 %add_convert_fusion = bf16[256,128,96]{1,2,0:T(8,128)(2,1)} fusion(f32[256,128,96]{1,2,0:T(8,128)} %fusion.25, f32[256,128,96]{1,2,0:T(8,128)} %fusion.43, bf16[256,96,96]{2,1,0:T(8,128)(2,1)} %copy.32, bf16[128,256,96]{0,2,1:T(8,128)(2,1)} %get-tuple-element.15), kind=kOutput, calls=%fused_computation.5 | convolution fusion | flops 613416960 | bytes 42467328 | tf_op jit(solution)/shard_map/cnb,nab->cna/dot_general | solution.py:54
  384.1 7.2 %fusion.41 = f32[128,128]{1,0:T(8,128)} fusion(bf16[128,24576]{1,0:T(8,128)(2,1)} %copy-done.1, bf16[128,24576]{0,1:T(8,128)(2,1)} %bitcast.63), kind=kOutput, calls=%fused_computation.69 | convolution fusion | flops 805306368 | bytes 12648448 | tf_op jit(solution)/shard_map/dot_general | solution.py:90
  391.3 9.3 %fusion.42 = f32[256,128,96]{1,2,0:T(8,128)} fusion(bf16[256,96,96]{2,1,0:T(8,128)(2,1)} %copy.33, bf16[128,256,96]{0,2,1:T(8,128)(2,1)S(1)} %bitcast.62), kind=kOutput, calls=%fused_computation.70 | convolution fusion | flops 603979776 | bytes 23592960 | tf_op jit(solution)/shard_map/cnb,nab->cna/dot_general | solution.py:54
  400.6 9.1 %fusion.23 = f32[256,128,96]{1,2,0:T(8,128)} fusion(bf16[256,96,96]{2,1,0:T(8,128)(2,1)} %copy.29, bf16[128,260,96]{0,2,1:T(8,128)(2,1)S(1)} %bitcast.60), kind=kOutput, calls=%fused_computation.35 | convolution fusion | flops 603979776 | bytes 23592960 | tf_op jit(solution)/shard_map/cnb,nab->cna/dot_general | solution.py:54
  409.7 15.8 %add_convert_fusion.1 = bf16[256,128,96]{1,2,0:T(8,128)(2,1)} fusion(f32[256,128,96]{1,2,0:T(8,128)} %fusion.23, f32[256,128,96]{1,2,0:T(8,128)} %fusion.42, bf16[256,96,96]{2,1,0:T(8,128)(2,1)} %copy.34, bf16[128,256,96]{0,2,1:T(8,128)(2,1)} %get-tuple-element.15), kind=kOutput, calls=%fused_computation.6 | convolution fusion | flops 613416960 | bytes 42467328 | tf_op jit(solution)/shard_map/cnb,nab->cna/dot_general | solution.py:54
  425.5 7.0 %fusion.40 = f32[128,128]{1,0:T(8,128)} fusion(bf16[128,24576]{1,0:T(8,128)(2,1)} %copy-done.1, bf16[128,24576]{0,1:T(8,128)(2,1)} %bitcast.65), kind=kOutput, calls=%fused_computation.68 | convolution fusion | flops 805306368 | bytes 12648448 | tf_op jit(solution)/shard_map/dot_general | solution.py:91
  432.5 7.4 %bitcast_convert_fusion = f32[1,128,24576]{1,2,0:T(8,128)} fusion(bf16[1,128,24576]{1,2,0:T(8,128)(2,1)} %bitcast.64), kind=kLoop, calls=%fused_computation.20 | loop fusion | flops 3145728 | bytes 18874368 | tf_op jit(solution)/shard_map/convert_element_type | solution.py:103
  439.9 0.0 all-reduce.6.cloned.1.call-update
  440.0 7.5 %bitcast_convert_fusion.1 = f32[1,128,24576]{1,2,0:T(8,128)} fusion(bf16[1,128,24576]{1,2,0:T(8,128)(2,1)} %bitcast.66), kind=kLoop, calls=%fused_computation.21 | loop fusion | flops 3145728 | bytes 18874368 | tf_op jit(solution)/shard_map/convert_element_type | solution.py:103
  447.4 12.6 %copy.27 = f32[1,128,24576]{2,1,0:T(8,128)} copy(f32[1,128,24576]{1,2,0:T(8,128)} %bitcast_convert_fusion) | data formatting | bytes 25165824 | tf_op jit(solution)/shard_map/convert_element_type | solution.py:103
  460.0 12.6 %copy.28 = f32[1,128,24576]{2,1,0:T(8,128)} copy(f32[1,128,24576]{1,2,0:T(8,128)} %bitcast_convert_fusion.1) | data formatting | bytes 25165824 | tf_op jit(solution)/shard_map/convert_element_type | solution.py:103
  472.6 3.0 all-reduce.6.cloned.1.call-done
  475.6 1.5 fusion.33
  477.1 1.2 gather_fusion
  478.4 1.2 gather_fusion.1
  479.6 11.8 %subtract_convert_fusion = bf16[1,128,24576]{2,1,0:T(8,128)(2,1)} fusion(f32[1,128,24576]{2,1,0:T(8,128)} %copy.28, f32[1,128,24576]{2,1,0:T(8,128)} %copy.27, f32[128]{0:T(128)S(1)} %divide_select_fusion), kind=kLoop, calls=%fused_computation.4 | loop fusion | flops 9437184 | bytes 31457792 | tf_op jit(solution)/shard_map/convert_element_type | solution.py:104
  (34 shorter events, 0.1 us)
Async XLA Ops:
  7.2 265.0 %all-reduce.4.cloned.1.call-start = ((), (), s32[]{:S(2)}) async-start(), calls=%async_computation | async-start | bytes 131072 | tf_op jit(solution)/shard_map/psum | solution.py:83
  16.3 2.6 copy-start.3
  18.9 13.8 %copy-start.5 = (s32[256,3]{0,1:T(4,128)S(1)}, s32[256,3]{0,1:T(4,128)}, u32[]{:S(2)}) copy-start(s32[256,3]{0,1:T(4,128)} %param.11) | copy-start | bytes 9220
  21.4 39.9 %collective-permute-start = (bf16[32,24576]{1,0:T(8,128)(2,1)}, bf16[32,24576]{1,0:T(8,128)(2,1)}, u32[]{:S(2)}, u32[]{:S(2)}) collective-permute-start(bf16[32,24576]{1,0:T(8,128)(2,1)} %get-tuple-element.22), channel_id=1, source_target_pairs={{0,8},{4,12},{8,16},{12,20},{16,24},{20,28},{1,9},{5,13},{9,17},{1... | collective-permute-start | bytes 4718600 | tf_op jit(solution)/shard_map/ppermute | solution.py:13
  27.5 35.4 %collective-permute-start.1 = (bf16[32,24576]{1,0:T(8,128)(2,1)}, bf16[32,24576]{1,0:T(8,128)(2,1)}, u32[]{:S(2)}, u32[]{:S(2)}) collective-permute-start(bf16[32,24576]{1,0:T(8,128)(2,1)} %get-tuple-element.22), channel_id=1, source_target_pairs={{0,4},{4,8},{8,12},{12,16},{16,20},{20,24},{24,28},{1,5},{5,9},{9,... | collective-permute-start | bytes 4718600 | tf_op jit(solution)/shard_map/ppermute | solution.py:13
  30.1 34.3 %collective-permute-start.2 = (bf16[32,24576]{1,0:T(8,128)(2,1)}, bf16[32,24576]{1,0:T(8,128)(2,1)S(1)}, u32[]{:S(2)}, u32[]{:S(2)}) collective-permute-start(bf16[32,24576]{1,0:T(8,128)(2,1)} %get-tuple-element.21), channel_id=1, source_target_pairs={{4,0},{8,4},{12,8},{16,12},{20,16},{24,20},{28,24},{5,1},{9,5},{13... | collective-permute-start | bytes 4718600 | tf_op jit(solution)/shard_map/ppermute | solution.py:13
  31.4 98.1 %collective-permute-start.3 = (bf16[32,24576]{1,0:T(8,128)(2,1)}, bf16[32,24576]{1,0:T(8,128)(2,1)S(1)}, u32[]{:S(2)}, u32[]{:S(2)}) collective-permute-start(bf16[32,24576]{1,0:T(8,128)(2,1)} %get-tuple-element.21), channel_id=1, source_target_pairs={{8,0},{12,4},{16,8},{20,12},{24,16},{28,20},{9,1},{13,5},{17,9},{2... | collective-permute-start | bytes 4718600 | tf_op jit(solution)/shard_map/ppermute | solution.py:13
  129.6 2.7 copy-start.4
  132.4 30.1 %collective-permute-start.4 = (bf16[128,192]{1,0:T(8,128)(2,1)S(1)}, bf16[128,192]{1,0:T(8,128)(2,1)S(1)}, u32[]{:S(2)}, u32[]{:S(2)}) collective-permute-start(bf16[128,192]{1,0:T(8,128)(2,1)S(1)} %get-tuple-element.20), channel_id=1, source_target_pairs={{0,1},{1,2},{2,3},{4,5},{5,6},{6,7},{8,9},{9,10},{10,11},{12,13},{... | collective-permute-start | bytes 147464 | tf_op jit(solution)/shard_map/ppermute | solution.py:24
  135.9 26.7 %collective-permute-start.5 = (bf16[128,192]{1,0:T(8,128)(2,1)S(1)}, bf16[128,192]{1,0:T(8,128)(2,1)S(1)}, u32[]{:S(2)}, u32[]{:S(2)}) collective-permute-start(bf16[128,192]{1,0:T(8,128)(2,1)S(1)} %get-tuple-element.19), channel_id=1, source_target_pairs={{1,0},{2,1},{3,2},{5,4},{6,5},{7,6},{9,8},{10,9},{11,10},{13,12},{... | collective-permute-start | bytes 147464 | tf_op jit(solution)/shard_map/ppermute | solution.py:26
  185.2 25.8 %slice-start.4 = ((s8[6291456]{0:T(1024)(128)(4,1)}), s8[4194304]{0:T(1024)(128)(4,1)S(1)}, s32[]{:S(2)}) async-start(s8[6291456]{0:T(1024)(128)(4,1)} %bitcast.67), calls=%async_computation.6 | async-start | bytes 8388608
  196.3 14.8 %slice-start.5 = ((s8[6291456]{0:T(1024)(128)(4,1)}), s8[2097152]{0:T(1024)(128)(4,1)S(1)}, s32[]{:S(2)}) async-start(s8[6291456]{0:T(1024)(128)(4,1)} %bitcast.67), calls=%async_computation.7 | async-start | bytes 4194304
  236.7 238.9 %all-reduce.6.cloned.1.call-start = ((), (), s32[]{:S(2)}) async-start(), calls=%async_computation.1 | async-start | bytes 262144 | tf_op jit(solution)/shard_map/psum | solution.py:92
  278.6 2.6 copy-start.1
  281.3 29.8 %collective-permute-start.6 = (bf16[128,192]{1,0:T(8,128)(2,1)S(1)}, bf16[128,192]{1,0:T(8,128)(2,1)S(1)}, u32[]{:S(2)}, u32[]{:S(2)}) collective-permute-start(bf16[128,192]{1,0:T(8,128)(2,1)S(1)} %get-tuple-element.18), channel_id=1, source_target_pairs={{0,1},{1,2},{2,3},{4,5},{5,6},{6,7},{8,9},{9,10},{10,11},{12,13},{... | collective-permute-start | bytes 147464 | tf_op jit(solution)/shard_map/ppermute | solution.py:24
  284.7 26.5 %collective-permute-start.7 = (bf16[128,192]{1,0:T(8,128)(2,1)S(1)}, bf16[128,192]{1,0:T(8,128)(2,1)S(1)}, u32[]{:S(2)}, u32[]{:S(2)}) collective-permute-start(bf16[128,192]{1,0:T(8,128)(2,1)S(1)} %get-tuple-element.17), channel_id=1, source_target_pairs={{1,0},{2,1},{3,2},{5,4},{6,5},{7,6},{9,8},{10,9},{11,10},{13,12},{... | collective-permute-start | bytes 147464 | tf_op jit(solution)/shard_map/ppermute | solution.py:26
  333.9 13.8 %copy-start = (bf16[128,24960]{0,1:T(8,128)(2,1)S(1)}, bf16[128,24960]{0,1:T(8,128)(2,1)}, u32[]{:S(2)}) copy-start(bf16[128,24960]{0,1:T(8,128)(2,1)} %copy.23) | copy-start | bytes 19169284
  347.7 11.4 %copy-start.2 = (bf16[128,256,96]{0,2,1:T(8,128)(2,1)}, bf16[128,256,96]{0,2,1:T(8,128)(2,1)S(1)}, u32[]{:S(2)}) copy-start(bf16[128,256,96]{0,2,1:T(8,128)(2,1)S(1)} %get-tuple-element.16) | copy-start | bytes 18874372
  384.1 7.2 %slice-start.2 = ((s8[6291456]{0:T(1024)(128)(4,1)}), s8[4194304]{0:T(1024)(128)(4,1)S(1)}, s32[]{:S(2)}) async-start(s8[6291456]{0:T(1024)(128)(4,1)} %bitcast.61), calls=%async_computation.4 | async-start | bytes 8388608
  384.1 7.2 %slice-start.3 = ((s8[6291456]{0:T(1024)(128)(4,1)}), s8[2097152]{0:T(1024)(128)(4,1)S(1)}, s32[]{:S(2)}) async-start(s8[6291456]{0:T(1024)(128)(4,1)} %bitcast.61), calls=%async_computation.5 | async-start | bytes 4194304
  384.1 16.5 %slice-start = ((s8[6389760]{0:T(1024)(128)(4,1)}), s8[4194304]{0:T(1024)(128)(4,1)S(1)}, s32[]{:S(2)}) async-start(s8[6389760]{0:T(1024)(128)(4,1)} %bitcast.58), calls=%async_computation.2 | async-start | bytes 8388608
  391.3 9.3 %slice-start.1 = ((s8[6389760]{0:T(1024)(128)(4,1)}), s8[2195456]{0:T(1024)(128)(4,1)S(1)}, s32[]{:S(2)}) async-start(s8[6389760]{0:T(1024)(128)(4,1)} %bitcast.58), calls=%async_computation.3 | async-start | bytes 4390912
Sparse Core Ops, SparseCore 0:
  236.8 35.3 all-reduce.3
  440.1 35.4 all-reduce.5
where the time goes:
time: 501 us; the launch traced here: 498 us
  local copies, waits for them, and re-layouts  160 us (32%)
  matrix products  143 us (29%)
  waiting for transfers between devices  110 us (22%)
  other arithmetic  45.3 us (9%)
  starting transfers between devices  20.9 us (4%)
  between operations  18.8 us (4%)
    dot_general x9, matrix products, block_product(): jnp.einsum('cnb,nab->cna', picked_all[column_slot], part_blocks, preferre...  115 us
    ppermute x4, waiting for transfers between devices, from_behind(): return lax.ppermute(block, axis, route)  82.8 us
    unnamed x33, local copies, waits for them, and re-layouts  61.5 us
    concatenate x4, local copies, waits for them, and re-layouts, padded_2(): jnp.concatenate([lax.ppermute(tail, axis, [(i, (i + 1) % count) for i in...  45.4 us
    psum x1, waiting for transfers between devices, shards(): margin = lax.psum(partial_margin, 'row') / NMAT  24.5 us
    slice x2, local copies, waits for them, and re-layouts, block_product(): blocks[:, :, column_slot * size_block:(column_slot + 1) * size_block]  21.6 us
    select_n x1, other arithmetic, block_product(): picked = jnp.where(hit, view, picked)  13.8 us
    convert_element_type x1, local copies, waits for them, and re-layouts, shards(): energy_cleaned.astype(jnp.float32)  12.6 us
  transfers between devices with their start and end apart: 10, of which 4 were waited for; matrix products, arithmetic and copies ran while one was open for 22% of the time, Pallas kernels for 0%

commit v1 on v0

--- a/solution.py
+++ b/solution.py
@@ -5,6 +5,12 @@
 
 NMAT = 98304
 WIN = 32
+
+
+def summed_here(x, axis):
+    terms = lax.all_gather(x, axis, axis=0, tiled=False)
+    acc = terms.sum(axis=0)
+    return acc
 
 
 def from_behind(block, axis, distance):
@@ -80,7 +86,7 @@
     padded_windows = padded_2(windows, (("row", 1),), rim_width)
     margin_windows = block_product((margin_blocks,), shifts, padded_windows)[0]
     partial_margin = jnp.dot(margin_windows, masked.T, preferred_element_type=jnp.float32)
-    margin = lax.psum(partial_margin, "row") / NMAT
+    margin = summed_here(partial_margin, "row") / NMAT
     removed = jnp.dot(margin.astype(jnp.bfloat16).T, windows, preferred_element_type=jnp.float32)
     cleaned = (masked.astype(jnp.float32) - removed).astype(jnp.bfloat16)
     padded_cleaned = padded_2(cleaned, (("row", 1),), rim_width)

time: 501 us -> 481 us (0.960)
  waiting for transfers between devices: 110 us -> 76.4 us
  blocking collectives: 0 us -> 15.5 us
    psum x1 -> x0, waiting for transfers between devices: 24.5 us -> none  [shards(): margin = lax.psum(partial_margin, 'row') / NMAT]
    all_gather x0 -> x1, blocking collectives: none -> 15.5 us  [summed_here(): terms = lax.all_gather(x, axis, axis=0, tiled=False)]
    ppermute x4, waiting for transfers between devices: 82.8 us -> 73.2 us  [from_behind(): return lax.ppermute(block, axis, route)]
    unnamed x33 -> x41, local copies, waits for them, and re-layouts: 61.5 us -> 65.2 us
  transfers between devices with their start and end apart: 10 -> 9, of which waited for: 4 -> 3; matrix products, arithmetic and copies ran while one was open for 22% -> 22% of each run, Pallas kernels for 0% -> 0%
where the time goes in v1:
time: 481 us; the launch traced here: 478 us
  local copies, waits for them, and re-layouts  159 us (33%)
  matrix products  142 us (30%)
  waiting for transfers between devices  76.4 us (16%)
  other arithmetic  45.2 us (9%)
  starting transfers between devices  20.7 us (4%)
  between operations  18.9 us (4%)
  blocking collectives  15.5 us (3%)
    dot_general x9, matrix products, block_product(): jnp.einsum('cnb,nab->cna', picked_all[column_slot], part_blocks, preferre...  115 us
    ppermute x4, waiting for transfers between devices, from_behind(): return lax.ppermute(block, axis, route)  73.2 us
    unnamed x41, local copies, waits for them, and re-layouts  65.2 us
    concatenate x4, local copies, waits for them, and re-layouts, padded_2(): jnp.concatenate([lax.ppermute(tail, axis, [(i, (i + 1) % count) for i in...  45.4 us
    slice x2, local copies, waits for them, and re-layouts, block_product(): blocks[:, :, column_slot * size_block:(column_slot + 1) * size_block]  17 us
    all_gather x1, blocking collectives, summed_here(): terms = lax.all_gather(x, axis, axis=0, tiled=False)  15.5 us
    select_n x1, other arithmetic, block_product(): picked = jnp.where(hit, view, picked)  13.8 us
    convert_element_type x1, local copies, waits for them, and re-layouts, shards(): energy_cleaned.astype(jnp.float32)  12.7 us
  transfers between devices with their start and end apart: 9, of which 3 were waited for; matrix products, arithmetic and copies ran while one was open for 22% of the time, Pallas kernels for 0%

profile of v1, /device:TPU:0, one launch (start us, length us, event | category | flops | bytes accessed | tf_op | source)
XLA Modules:
  0.0 478.2 jit_solution(10399807190659105332)
XLA Ops:
  7.2 0.0 all-reduce.3.cloned.1.call-start
  7.2 1.3 fusion.39
  13.1 3.3 bitcast_select_fusion
  16.3 2.7 copy-done.3
  19.0 2.5 constant_dynamic-slice_fusion
  21.5 6.0 %collective-permute-start = (bf16[32,24576]{1,0:T(8,128)(2,1)}, bf16[32,24576]{1,0:T(8,128)(2,1)}, u32[]{:S(2)}, u32[]{:S(2)}) collective-permute-start(bf16[32,24576]{1,0:T(8,128)(2,1)} %get-tuple-element.22), channel_id=1, source_target_pairs={{0,8},{4,12},{8,16},{12,20},{16,24},{20,28},{1,9},{5,13},{9,17},{1... | collective-permute-start | bytes 4718600 | tf_op jit(solution)/shard_map/ppermute | solution.py:19
  27.5 2.7 collective-permute-start.1
  30.2 1.3 collective-permute-start.2
  31.5 1.3 collective-permute-start.3
  32.8 0.0 slice-start.7
  32.8 11.9 %fusion.36 = (bf16[256,96,96]{0,2,1:T(8,128)(2,1)}, bf16[256,96,96]{0,2,1:T(8,128)(2,1)}, bf16[256,96,96]{0,2,1:T(8,128)(2,1)}) fusion(bf16[256,96,288]{0,2,1:T(8,128)(2,1)} %param.9), kind=kLoop, calls=%fused_computation.64 | loop fusion | bytes 28311552 | tf_op jit(solution)/shard_map/slice | solution.py:59
  44.7 0.2 slice-done.8
  45.0 1.8 slice-done.9
  46.7 5.1 %fusion.35 = (bf16[256,96,96]{0,2,1:T(8,128)(2,1)}, bf16[256,96,96]{0,2,1:T(8,128)(2,1)}, bf16[256,96,96]{0,2,1:T(8,128)(2,1)}) fusion(bf16[256,96,288]{0,2,1:T(8,128)(2,1)S(1)} %bitcast.74), kind=kLoop, calls=%fused_computation.63 | loop fusion | bytes 28311552 | tf_op jit(solution)/shard_map/slice | solution.py:59
  51.8 9.6 %collective-permute-done = bf16[32,24576]{1,0:T(8,128)(2,1)} collective-permute-done((bf16[32,24576]{1,0:T(8,128)(2,1)}, bf16[32,24576]{1,0:T(8,128)(2,1)}, u32[]{:S(2)}, u32[]{:S(2)}) %collective-permute-start) | collective-permute-done | bytes 1572896 | tf_op jit(solution)/shard_map/ppermute | solution.py:19
  61.5 1.5 constant_dynamic-update-slice_fusion.3
  63.0 1.5 constant_dynamic-update-slice_fusion.2
  64.5 1.5 constant_dynamic-update-slice_fusion.1
  66.0 63.5 %collective-permute-done.3 = bf16[32,24576]{1,0:T(8,128)(2,1)S(1)} collective-permute-done((bf16[32,24576]{1,0:T(8,128)(2,1)}, bf16[32,24576]{1,0:T(8,128)(2,1)S(1)}, u32[]{:S(2)}, u32[]{:S(2)}) %collective-permute-start.3) | collective-permute-done | bytes 1572896 | tf_op jit(solution)/shard_map/ppermute | solution.py:19
  129.6 0.1 constant_dynamic-update-slice_fusion
  129.7 0.0 copy-start.4
  129.7 2.7 copy-done.4
  132.4 0.1 fusion.38
  132.5 3.5 collective-permute-start.4
  136.0 1.3 collective-permute-start.5
  137.3 8.5 %copy.31 = bf16[256,96,96]{2,1,0:T(8,128)(2,1)} copy(bf16[256,96,96]{0,2,1:T(8,128)(2,1)} %get-tuple-element.13) | data formatting | bytes 9437184
  145.8 8.4 %copy.30 = bf16[256,96,96]{2,1,0:T(8,128)(2,1)} copy(bf16[256,96,96]{0,2,1:T(8,128)(2,1)} %get-tuple-element.14) | data formatting | bytes 9437184
  154.2 8.5 %copy.32 = bf16[256,96,96]{2,1,0:T(8,128)(2,1)} copy(bf16[256,96,96]{0,2,1:T(8,128)(2,1)} %get-tuple-element.12) | data formatting | bytes 9437184
  162.6 13.5 %concatenate.15 = bf16[128,24960]{1,0:T(8,128)(2,1)} concatenate(bf16[128,192]{1,0:T(8,128)(2,1)S(1)} %collective-permute-done.4, bf16[128,24576]{1,0:T(8,128)(2,1)} %copy-done.4, bf16[128,192]{1,0:T(8,128)(2,1)S(1)} %collective-permute-done.5), dimensions={1} | concatenate | bytes 12779520 | tf_op jit(solution)/shard_map/concatenate | solution.py:28
  176.1 9.2 %copy.19 = bf16[128,24960]{0,1:T(8,128)(2,1)} copy(bf16[128,24960]{1,0:T(8,128)(2,1)} %concatenate.15) | data formatting | bytes 12779520 | tf_op jit(solution)/shard_map/concatenate | solution.py:28
  185.3 11.0 %fusion.21 = f32[256,128,96]{1,2,0:T(8,128)} fusion(bf16[256,96,96]{2,1,0:T(8,128)(2,1)} %copy.30, bf16[128,260,96]{0,2,1:T(8,128)(2,1)} %bitcast.70), kind=kOutput, calls=%fused_computation.33 | convolution fusion | flops 603979776 | bytes 25165824 | tf_op jit(solution)/shard_map/cnb,nab->cna/dot_general | solution.py:60
  196.4 14.8 %fusion.8 = f32[256,128,96]{1,2,0:T(8,128)} fusion(bf16[256,96,96]{2,1,0:T(8,128)(2,1)} %copy.31, bf16[128,260,96]{0,2,1:T(8,128)(2,1)} %bitcast.71, pred[256]{0:T(512)(128)(4,1)S(1)} %get-tuple-element.4, pred[256]{0:T(512)(128)(4,1)S(1)} %get-tuple-element.6), kind=kOutput, calls=%fused_computation.18 | convolution fusion | flops 610271232 | bytes 37749248 | tf_op jit(solution)/shard_map/cnb,nab->cna/dot_general | solution.py:60
  211.2 18.5 %add_convert_fusion.2 = bf16[256,128,96]{1,2,0:T(8,128)(2,1)} fusion(f32[256,128,96]{1,2,0:T(8,128)} %fusion.21, f32[256,128,96]{1,2,0:T(8,128)} %fusion.8, bf16[256,96,96]{2,1,0:T(8,128)(2,1)S(1)} %bitcast.69, bf16[128,260,96]{0,2,1:T(8,128)(2,1)} %bitcast.72, pred[256]{0:T(512)(128)(4,1)S(1)} %get-tuple-element.5, pred[256]{0:T(512)(128)(4,1)S(1)} %get-tuple-element.3), kind=kOutput, calls=%fused_computation.7 | convolution fusion | flops 619708416 | bytes 55050752 | tf_op jit(solution)/shard_map/cnb,nab->cna/dot_general | solution.py:60
  229.6 6.5 %fusion.11 = f32[128,128]{1,0:T(8,128)S(1)} fusion(bf16[128,24576]{0,1:T(8,128)(2,1)} %bitcast.75, bf16[1,128,24576]{2,1,0:T(8,128)(2,1)} %param.6, pred[128]{0:T(512)(128)(4,1)S(1)} %iota_compare_fusion), kind=kOutput, calls=%fused_computation.22 | convolution fusion | flops 808452096 | bytes 12648576 | tf_op jit(solution)/shard_map/dot_general | solution.py:88
  236.2 15.5 %all-gather = f32[512,128]{1,0:T(8,128)S(1)} all-gather(f32[128,128]{1,0:T(8,128)S(1)} %fusion.11), channel_id=2, replica_groups=mesh['cuts'=8,'row'=4] {'row'}, dimensions={0}, use_global_device_ids=true | all-gather | bytes 327680 | tf_op jit(solution)/shard_map/all_gather | solution.py:11
  251.6 6.4 %fusion = bf16[128,24576]{1,0:T(8,128)(2,1)S(1)} fusion(bf16[128,24576]{1,0:T(8,128)(2,1)} %copy-done.4, bf16[128,24576]{1,0:T(8,128)(2,1)} %copy-done.3, f32[128,128]{1,0:T(8,128)S(1)} %reduce_sum.9), kind=kOutput, calls=%fused_computation.3 | convolution fusion | flops 814776320 | bytes 18939904 | tf_op jit(solution)/shard_map/dot_general | solution.py:90
  258.1 2.7 copy-done.1
  260.8 0.1 fusion.37
  260.9 3.4 collective-permute-start.6
  264.3 1.3 collective-permute-start.7
  265.6 8.5 %copy.33 = bf16[256,96,96]{2,1,0:T(8,128)(2,1)} copy(bf16[256,96,96]{0,2,1:T(8,128)(2,1)} %get-tuple-element.10) | data formatting | bytes 9437184
  274.1 8.3 %copy.29 = bf16[256,96,96]{2,1,0:T(8,128)(2,1)} copy(bf16[256,96,96]{0,2,1:T(8,128)(2,1)} %get-tuple-element.11) | data formatting | bytes 9437184
  282.4 8.5 %copy.34 = bf16[256,96,96]{2,1,0:T(8,128)(2,1)} copy(bf16[256,96,96]{0,2,1:T(8,128)(2,1)} %get-tuple-element.9) | data formatting | bytes 9437184
  290.9 13.5 %concatenate.16 = bf16[128,24960]{1,0:T(8,128)(2,1)} concatenate(bf16[128,192]{1,0:T(8,128)(2,1)S(1)} %collective-permute-done.6, bf16[128,24576]{1,0:T(8,128)(2,1)} %copy-done.1, bf16[128,192]{1,0:T(8,128)(2,1)S(1)} %collective-permute-done.7), dimensions={1} | concatenate | bytes 12779520 | tf_op jit(solution)/shard_map/concatenate | solution.py:28
  304.4 9.2 %copy.23 = bf16[128,24960]{0,1:T(8,128)(2,1)} copy(bf16[128,24960]{1,0:T(8,128)(2,1)} %concatenate.16) | data formatting | bytes 12779520 | tf_op jit(solution)/shard_map/concatenate | solution.py:28
  313.6 13.8 %fusion.1 = (bf16[128,256,96]{0,2,1:T(8,128)(2,1)}, bf16[128,256,96]{0,2,1:T(8,128)(2,1)S(1)}) fusion(bf16[128,260,96]{0,2,1:T(8,128)(2,1)} %bitcast.57, pred[256]{0:T(512)(128)(4,1)S(1)} %get-tuple-element.5, pred[256]{0:T(512)(128)(4,1)S(1)} %get-tuple-element.3, pred[256]{0:T(512)(128)(4,1)S(1)} %get-tuple-element.4, pred[256]{0:T(512)(128)(4,1)S(1)} %get-tuple-element.6), kind=kLoop, calls=%fused_computation.9 | loop fusion | flops 12582912 | bytes 44041216 | tf_op jit(solution)/shard_map/jit(_where)/select_n | solution.py:53
  327.3 11.4 %fusion.25 = f32[256,128,96]{1,2,0:T(8,128)} fusion(bf16[256,96,96]{2,1,0:T(8,128)(2,1)} %copy.30, bf16[128,260,96]{0,2,1:T(8,128)(2,1)S(1)} %bitcast.58), kind=kOutput, calls=%fused_computation.37 | convolution fusion | flops 603979776 | bytes 23592960 | tf_op jit(solution)/shard_map/cnb,nab->cna/dot_general | solution.py:60
  338.8 9.2 %fusion.43 = f32[256,128,96]{1,2,0:T(8,128)} fusion(bf16[256,96,96]{2,1,0:T(8,128)(2,1)} %copy.31, bf16[128,256,96]{0,2,1:T(8,128)(2,1)S(1)} %get-tuple-element.16), kind=kOutput, calls=%fused_computation.71 | convolution fusion | flops 603979776 | bytes 23592960 | tf_op jit(solution)/shard_map/cnb,nab->cna/dot_general | solution.py:60
  347.9 15.8 %add_convert_fusion = bf16[256,128,96]{1,2,0:T(8,128)(2,1)} fusion(f32[256,128,96]{1,2,0:T(8,128)} %fusion.25, f32[256,128,96]{1,2,0:T(8,128)} %fusion.43, bf16[256,96,96]{2,1,0:T(8,128)(2,1)} %copy.32, bf16[128,256,96]{0,2,1:T(8,128)(2,1)} %get-tuple-element.15), kind=kOutput, calls=%fused_computation.5 | convolution fusion | flops 613416960 | bytes 42467328 | tf_op jit(solution)/shard_map/cnb,nab->cna/dot_general | solution.py:60
  363.7 7.2 %fusion.41 = f32[128,128]{1,0:T(8,128)} fusion(bf16[128,24576]{1,0:T(8,128)(2,1)} %copy-done.1, bf16[128,24576]{0,1:T(8,128)(2,1)} %bitcast.64), kind=kOutput, calls=%fused_computation.69 | convolution fusion | flops 805306368 | bytes 12648448 | tf_op jit(solution)/shard_map/dot_general | solution.py:96
  370.9 9.3 %fusion.42 = f32[256,128,96]{1,2,0:T(8,128)} fusion(bf16[256,96,96]{2,1,0:T(8,128)(2,1)} %copy.33, bf16[128,256,96]{0,2,1:T(8,128)(2,1)S(1)} %bitcast.63), kind=kOutput, calls=%fused_computation.70 | convolution fusion | flops 603979776 | bytes 23592960 | tf_op jit(solution)/shard_map/cnb,nab->cna/dot_general | solution.py:60
  380.2 9.1 %fusion.23 = f32[256,128,96]{1,2,0:T(8,128)} fusion(bf16[256,96,96]{2,1,0:T(8,128)(2,1)} %copy.29, bf16[128,260,96]{0,2,1:T(8,128)(2,1)S(1)} %bitcast.61), kind=kOutput, calls=%fused_computation.35 | convolution fusion | flops 603979776 | bytes 23592960 | tf_op jit(solution)/shard_map/cnb,nab->cna/dot_general | solution.py:60
  389.3 15.8 %add_convert_fusion.1 = bf16[256,128,96]{1,2,0:T(8,128)(2,1)} fusion(f32[256,128,96]{1,2,0:T(8,128)} %fusion.23, f32[256,128,96]{1,2,0:T(8,128)} %fusion.42, bf16[256,96,96]{2,1,0:T(8,128)(2,1)} %copy.34, bf16[128,256,96]{0,2,1:T(8,128)(2,1)} %get-tuple-element.15), kind=kOutput, calls=%fused_computation.6 | convolution fusion | flops 613416960 | bytes 42467328 | tf_op jit(solution)/shard_map/cnb,nab->cna/dot_general | solution.py:60
  405.1 7.0 %fusion.40 = f32[128,128]{1,0:T(8,128)} fusion(bf16[128,24576]{1,0:T(8,128)(2,1)} %copy-done.1, bf16[128,24576]{0,1:T(8,128)(2,1)} %bitcast.66), kind=kOutput, calls=%fused_computation.68 | convolution fusion | flops 805306368 | bytes 12648448 | tf_op jit(solution)/shard_map/dot_general | solution.py:97
  412.2 7.4 %bitcast_convert_fusion = f32[1,128,24576]{1,2,0:T(8,128)} fusion(bf16[1,128,24576]{1,2,0:T(8,128)(2,1)} %bitcast.65), kind=kLoop, calls=%fused_computation.20 | loop fusion | flops 3145728 | bytes 18874368 | tf_op jit(solution)/shard_map/convert_element_type | solution.py:109
  419.6 0.0 all-reduce.3.cloned.1.call-update
  419.6 7.4 %bitcast_convert_fusion.1 = f32[1,128,24576]{1,2,0:T(8,128)} fusion(bf16[1,128,24576]{1,2,0:T(8,128)(2,1)} %bitcast.67), kind=kLoop, calls=%fused_computation.21 | loop fusion | flops 3145728 | bytes 18874368 | tf_op jit(solution)/shard_map/convert_element_type | solution.py:109
  427.0 12.6 %copy.27 = f32[1,128,24576]{2,1,0:T(8,128)} copy(f32[1,128,24576]{1,2,0:T(8,128)} %bitcast_convert_fusion) | data formatting | bytes 25165824 | tf_op jit(solution)/shard_map/convert_element_type | solution.py:109
  439.6 12.7 %copy.28 = f32[1,128,24576]{2,1,0:T(8,128)} copy(f32[1,128,24576]{1,2,0:T(8,128)} %bitcast_convert_fusion.1) | data formatting | bytes 25165824 | tf_op jit(solution)/shard_map/convert_element_type | solution.py:109
  452.3 3.2 all-reduce.3.cloned.1.call-done
  455.5 1.5 fusion.33
  457.1 1.2 gather_fusion
  458.3 1.2 gather_fusion.1
  459.6 11.8 %subtract_convert_fusion = bf16[1,128,24576]{2,1,0:T(8,128)(2,1)} fusion(f32[1,128,24576]{2,1,0:T(8,128)} %copy.28, f32[1,128,24576]{2,1,0:T(8,128)} %copy.27, f32[128]{0:T(128)S(1)} %divide_select_fusion), kind=kLoop, calls=%fused_computation.4 | loop fusion | flops 9437184 | bytes 31457792 | tf_op jit(solution)/shard_map/convert_element_type | solution.py:110
  (42 shorter events, 0.1 us)
Async XLA Ops:
  7.2 448.4 %all-reduce.3.cloned.1.call-start = ((), (), s32[]{:S(2)}) async-start(), calls=%async_computation | async-start | bytes 262144 | tf_op jit(solution)/shard_map/psum | solution.py:98
  16.3 2.7 copy-start.3
  19.0 13.7 %copy-start.5 = (s32[256,3]{0,1:T(4,128)S(1)}, s32[256,3]{0,1:T(4,128)}, u32[]{:S(2)}) copy-start(s32[256,3]{0,1:T(4,128)} %param.11) | copy-start | bytes 9220
  19.0 25.7 %slice-start.6 = ((s8[14155776]{0:T(1024)(128)(4,1)}), s8[1572864]{0:T(1024)(128)(4,1)S(1)}, s32[]{:S(2)}) async-start(s8[14155776]{0:T(1024)(128)(4,1)} %bitcast.73), calls=%async_computation.7 | async-start | bytes 3145728
  21.5 39.9 %collective-permute-start = (bf16[32,24576]{1,0:T(8,128)(2,1)}, bf16[32,24576]{1,0:T(8,128)(2,1)}, u32[]{:S(2)}, u32[]{:S(2)}) collective-permute-start(bf16[32,24576]{1,0:T(8,128)(2,1)} %get-tuple-element.22), channel_id=1, source_target_pairs={{0,8},{4,12},{8,16},{12,20},{16,24},{20,28},{1,9},{5,13},{9,17},{1... | collective-permute-start | bytes 4718600 | tf_op jit(solution)/shard_map/ppermute | solution.py:19
  27.5 35.5 %collective-permute-start.1 = (bf16[32,24576]{1,0:T(8,128)(2,1)}, bf16[32,24576]{1,0:T(8,128)(2,1)}, u32[]{:S(2)}, u32[]{:S(2)}) collective-permute-start(bf16[32,24576]{1,0:T(8,128)(2,1)} %get-tuple-element.22), channel_id=1, source_target_pairs={{0,4},{4,8},{8,12},{12,16},{16,20},{20,24},{24,28},{1,5},{5,9},{9,... | collective-permute-start | bytes 4718600 | tf_op jit(solution)/shard_map/ppermute | solution.py:19
  30.2 34.3 %collective-permute-start.2 = (bf16[32,24576]{1,0:T(8,128)(2,1)}, bf16[32,24576]{1,0:T(8,128)(2,1)}, u32[]{:S(2)}, u32[]{:S(2)}) collective-permute-start(bf16[32,24576]{1,0:T(8,128)(2,1)} %get-tuple-element.21), channel_id=1, source_target_pairs={{4,0},{8,4},{12,8},{16,12},{20,16},{24,20},{28,24},{5,1},{9,5},{13... | collective-permute-start | bytes 4718600 | tf_op jit(solution)/shard_map/ppermute | solution.py:19
  31.5 98.1 %collective-permute-start.3 = (bf16[32,24576]{1,0:T(8,128)(2,1)}, bf16[32,24576]{1,0:T(8,128)(2,1)S(1)}, u32[]{:S(2)}, u32[]{:S(2)}) collective-permute-start(bf16[32,24576]{1,0:T(8,128)(2,1)} %get-tuple-element.21), channel_id=1, source_target_pairs={{8,0},{12,4},{16,8},{20,12},{24,16},{28,20},{9,1},{13,5},{17,9},{2... | collective-permute-start | bytes 4718600 | tf_op jit(solution)/shard_map/ppermute | solution.py:19
  32.8 11.9 %slice-start.7 = ((s8[14155776]{0:T(1024)(128)(4,1)}), s8[4194304]{0:T(1024)(128)(4,1)S(1)}, s32[]{:S(2)}) async-start(s8[14155776]{0:T(1024)(128)(4,1)} %bitcast.73), calls=%async_computation.8 | async-start | bytes 8388608
  32.8 12.1 %slice-start.8 = ((s8[14155776]{0:T(1024)(128)(4,1)}), s8[4194304]{0:T(1024)(128)(4,1)S(1)}, s32[]{:S(2)}) async-start(s8[14155776]{0:T(1024)(128)(4,1)} %bitcast.73), calls=%async_computation.9 | async-start | bytes 8388608
  32.8 13.9 %slice-start.9 = ((s8[14155776]{0:T(1024)(128)(4,1)}), s8[4194304]{0:T(1024)(128)(4,1)S(1)}, s32[]{:S(2)}) async-start(s8[14155776]{0:T(1024)(128)(4,1)} %bitcast.73), calls=%async_computation.10 | async-start | bytes 8388608
  129.7 2.7 copy-start.4
  132.5 30.2 %collective-permute-start.4 = (bf16[128,192]{1,0:T(8,128)(2,1)S(1)}, bf16[128,192]{1,0:T(8,128)(2,1)S(1)}, u32[]{:S(2)}, u32[]{:S(2)}) collective-permute-start(bf16[128,192]{1,0:T(8,128)(2,1)S(1)} %get-tuple-element.20), channel_id=1, source_target_pairs={{0,1},{1,2},{2,3},{4,5},{5,6},{6,7},{8,9},{9,10},{10,11},{12,13},{... | collective-permute-start | bytes 147464 | tf_op jit(solution)/shard_map/ppermute | solution.py:30
  136.0 26.7 %collective-permute-start.5 = (bf16[128,192]{1,0:T(8,128)(2,1)S(1)}, bf16[128,192]{1,0:T(8,128)(2,1)S(1)}, u32[]{:S(2)}, u32[]{:S(2)}) collective-permute-start(bf16[128,192]{1,0:T(8,128)(2,1)S(1)} %get-tuple-element.19), channel_id=1, source_target_pairs={{1,0},{2,1},{3,2},{5,4},{6,5},{7,6},{9,8},{10,9},{11,10},{13,12},{... | collective-permute-start | bytes 147464 | tf_op jit(solution)/shard_map/ppermute | solution.py:32
  185.3 25.8 %slice-start.4 = ((s8[6291456]{0:T(1024)(128)(4,1)}), s8[4194304]{0:T(1024)(128)(4,1)S(1)}, s32[]{:S(2)}) async-start(s8[6291456]{0:T(1024)(128)(4,1)} %bitcast.68), calls=%async_computation.5 | async-start | bytes 8388608
  196.4 14.8 %slice-start.5 = ((s8[6291456]{0:T(1024)(128)(4,1)}), s8[2097152]{0:T(1024)(128)(4,1)S(1)}, s32[]{:S(2)}) async-start(s8[6291456]{0:T(1024)(128)(4,1)} %bitcast.68), calls=%async_computation.6 | async-start | bytes 4194304
  258.1 2.7 copy-start.1
  260.9 30.0 %collective-permute-start.6 = (bf16[128,192]{1,0:T(8,128)(2,1)S(1)}, bf16[128,192]{1,0:T(8,128)(2,1)S(1)}, u32[]{:S(2)}, u32[]{:S(2)}) collective-permute-start(bf16[128,192]{1,0:T(8,128)(2,1)S(1)} %get-tuple-element.18), channel_id=1, source_target_pairs={{0,1},{1,2},{2,3},{4,5},{5,6},{6,7},{8,9},{9,10},{10,11},{12,13},{... | collective-permute-start | bytes 147464 | tf_op jit(solution)/shard_map/ppermute | solution.py:30
  264.3 26.6 %collective-permute-start.7 = (bf16[128,192]{1,0:T(8,128)(2,1)S(1)}, bf16[128,192]{1,0:T(8,128)(2,1)S(1)}, u32[]{:S(2)}, u32[]{:S(2)}) collective-permute-start(bf16[128,192]{1,0:T(8,128)(2,1)S(1)} %get-tuple-element.17), channel_id=1, source_target_pairs={{1,0},{2,1},{3,2},{5,4},{6,5},{7,6},{9,8},{10,9},{11,10},{13,12},{... | collective-permute-start | bytes 147464 | tf_op jit(solution)/shard_map/ppermute | solution.py:32
  313.6 13.8 %copy-start = (bf16[128,24960]{0,1:T(8,128)(2,1)S(1)}, bf16[128,24960]{0,1:T(8,128)(2,1)}, u32[]{:S(2)}) copy-start(bf16[128,24960]{0,1:T(8,128)(2,1)} %copy.23) | copy-start | bytes 19169284
  327.3 11.4 %copy-start.2 = (bf16[128,256,96]{0,2,1:T(8,128)(2,1)}, bf16[128,256,96]{0,2,1:T(8,128)(2,1)S(1)}, u32[]{:S(2)}) copy-start(bf16[128,256,96]{0,2,1:T(8,128)(2,1)S(1)} %get-tuple-element.16) | copy-start | bytes 18874372
  363.7 7.2 %slice-start.2 = ((s8[6291456]{0:T(1024)(128)(4,1)}), s8[4194304]{0:T(1024)(128)(4,1)S(1)}, s32[]{:S(2)}) async-start(s8[6291456]{0:T(1024)(128)(4,1)} %bitcast.62), calls=%async_computation.3 | async-start | bytes 8388608
  363.7 7.2 %slice-start.3 = ((s8[6291456]{0:T(1024)(128)(4,1)}), s8[2097152]{0:T(1024)(128)(4,1)S(1)}, s32[]{:S(2)}) async-start(s8[6291456]{0:T(1024)(128)(4,1)} %bitcast.62), calls=%async_computation.4 | async-start | bytes 4194304
  363.7 16.5 %slice-start = ((s8[6389760]{0:T(1024)(128)(4,1)}), s8[4194304]{0:T(1024)(128)(4,1)S(1)}, s32[]{:S(2)}) async-start(s8[6389760]{0:T(1024)(128)(4,1)} %bitcast.59), calls=%async_computation.1 | async-start | bytes 8388608
  370.9 9.3 %slice-start.1 = ((s8[6389760]{0:T(1024)(128)(4,1)}), s8[2195456]{0:T(1024)(128)(4,1)S(1)}, s32[]{:S(2)}) async-start(s8[6389760]{0:T(1024)(128)(4,1)} %bitcast.59), calls=%async_computation.2 | async-start | bytes 4390912
Sparse Core Ops, SparseCore 0:
  419.7 35.7 all-reduce.2
